TPU v7x, 32 devices: a whole 2x2x4 slice. The times are simulated.
32 devices in a mesh: ctx: 4 (over x, core), ep: 8 (over z, y).
Axes of the slice: x: 2, y: 2, z: 4, core: 2. Of those that a mesh axis runs over, the one named last changes fastest.
Arguments:
- query_latent: bfloat16 [1, 512, 128, 512], P(None, 'ctx', 'ep'), may hold values from -6 to 6
- query_rope: bfloat16 [1, 128, 64, 512], P(None, 'ep', None, 'ctx'), may hold values from -12 to 12
- key_latent: bfloat16 [1, 512, 512], P(None, 'ctx'), may hold values from -6 to 6
- key_rope: bfloat16 [1, 64, 512], P(None, None, 'ctx'), may hold values from -14 to 14
- output_grad: bfloat16 [1, 512, 128, 512], P(None, 'ctx', 'ep'), may hold values from -6 to 6
Outputs:
- attended: bfloat16 [1, 512, 128, 512], P(None, 'ctx', 'ep')
- query_latent_grad: bfloat16 [1, 512, 128, 512], P(None, 'ctx', 'ep')
- query_rope_grad: bfloat16 [1, 128, 64, 512], P(None, 'ep', None, 'ctx')
- key_latent_grad: bfloat16 [1, 512, 512], P(None, 'ctx')
- key_rope_grad: bfloat16 [1, 64, 512], P(None, None, 'ctx')
All inputs are finite; a program needn't handle non-finite values.
Results may differ from a plain program's by a relative error of at most 0.018.
Values may be sent and summed in bfloat16 or wider, within the bound.
No kernel may reach another device: no remote copies, remote signals or barrier semaphores. Data moves between devices by JAX's collectives and lax.ppermute only.
A program may use at most 64 MiB of HBM per device.

v0:
```python
import jax
import jax.numpy as jnp
from jax import lax
from jax.sharding import PartitionSpec as P

scale_factor = 192.0 ** (-0.5)


def causal_reduce_ctx(blocks, n_ctx):
    here = lax.axis_index("ctx")
    total = jnp.take(blocks, here, axis=0).astype(jnp.float32)
    for shift in range(1, n_ctx):
        sent = jnp.take(blocks, jnp.maximum(here - shift, 0), axis=0)
        got = lax.ppermute(sent, "ctx", [(i, i - shift) for i in range(shift, n_ctx)])
        total = total + got.astype(jnp.float32)
    return total


def butterfly_sum_ep(total, n_ep):
    if n_ep & n_ep - 1:
        return lax.psum(total.astype(jnp.bfloat16), "ep").astype(jnp.float32)
    bit = 1
    while bit < n_ep:
        mine = total.astype(jnp.bfloat16)
        theirs = lax.ppermute(mine, "ep", [(i, i ^ bit) for i in range(n_ep)])
        total = mine.astype(jnp.float32) + theirs.astype(jnp.float32)
        bit *= 2
    return total


def body(query_latent, query_rope, key_latent, key_rope, output_grad):
    n_ctx = lax.axis_size("ctx")
    n_ep = lax.axis_size("ep")
    block_len = query_latent.shape[1]
    kvr = key_latent.shape[2]
    local_keys = jnp.concatenate([key_latent[0], key_rope[0].T], axis=1)
    whole_keys = lax.all_gather(local_keys, "ctx", axis=0, tiled=True)
    whole_latent = whole_keys[None, :, :kvr]
    whole_rope = whole_keys[:, kvr:].T[None]
    length = whole_latent.shape[1]
    offset = lax.axis_index("ctx") * block_len
    query_place = offset + jnp.arange(block_len, dtype=jnp.int32)
    allowed = jnp.arange(length, dtype=jnp.int32)[None, :] <= query_place[:, None]
    scores = jnp.einsum(
        "sthd,sjd->shtj", query_latent, whole_latent, preferred_element_type=jnp.float32
    )
    scores = scores + jnp.einsum(
        "shdt,sdj->shtj", query_rope, whole_rope, preferred_element_type=jnp.float32
    )
    scores = jnp.where(allowed, scores * scale_factor, jnp.float32(-1e30))
    row_max = jnp.max(scores, axis=-1, keepdims=True)
    powers = jnp.exp(scores - row_max)
    weights = powers / jnp.sum(powers, axis=-1, keepdims=True)
    rounded_weights = weights.astype(jnp.bfloat16)
    attended = jnp.einsum(
        "shtj,sjd->sthd", rounded_weights, whole_latent, preferred_element_type=jnp.float32
    ).astype(jnp.bfloat16)
    row_dots = jnp.einsum(
        "sthd,sthd->sht", output_grad, attended, preferred_element_type=jnp.float32
    )
    weight_grad = jnp.einsum(
        "sthd,sjd->shtj", output_grad, whole_latent, preferred_element_type=jnp.float32
    )
    score_grad = (weights * (weight_grad - row_dots[..., None])).astype(jnp.bfloat16)
    latent_qgrad = (
        scale_factor
        * jnp.einsum("shtj,sjd->sthd", score_grad, whole_latent, preferred_element_type=jnp.float32)
    ).astype(jnp.bfloat16)
    rope_qgrad = (
        scale_factor
        * jnp.einsum("shtj,sdj->shdt", score_grad, whole_rope, preferred_element_type=jnp.float32)
    ).astype(jnp.bfloat16)
    latent_term = scale_factor * jnp.einsum(
        "shtj,sthd->jd", score_grad, query_latent, preferred_element_type=jnp.float32
    )
    latent_term = latent_term + jnp.einsum(
        "shtj,sthd->jd", rounded_weights, output_grad, preferred_element_type=jnp.float32
    )
    rope_term = scale_factor * jnp.einsum(
        "shtj,shdt->jd", score_grad, query_rope, preferred_element_type=jnp.float32
    )
    terms = jnp.concatenate([latent_term, rope_term], axis=1).astype(jnp.bfloat16)
    total = causal_reduce_ctx(terms.reshape(n_ctx, block_len, -1), n_ctx)
    total = butterfly_sum_ep(total, n_ep).astype(jnp.bfloat16)
    latent_kgrad = total[None, :, :kvr]
    rope_kgrad = total[:, kvr:].T[None]
    return (attended, latent_qgrad, rope_qgrad, latent_kgrad, rope_kgrad)


def solution(mesh):
    placed = (
        P(None, "ctx", "ep", None),
        P(None, "ep", None, "ctx"),
        P(None, "ctx", None),
        P(None, None, "ctx"),
        P(None, "ctx", "ep", None),
    )
    return jax.shard_map(
        body,
        mesh=mesh,
        in_specs=placed,
        out_specs=(
            P(None, "ctx", "ep", None),
            P(None, "ctx", "ep", None),
            P(None, "ep", None, "ctx"),
            P(None, "ctx", None),
            P(None, None, "ctx"),
        ),
        check_vma=False,
    )
```

profile of v0, /device:TPU:0, one launch (start us, length us, event | category | flops | bytes accessed | tf_op | source)
XLA Modules:
  0.0 93.7 jit_solution(13140443794704222318)
XLA Ops:
  2.6 9.3 %all_gather.3 = bf16[512,576]{1,0:T(8,128)(2,1)S(1)} all-gather(bf16[128,576]{1,0:T(8,128)(2,1)S(1)} %pad_maximum_fusion), channel_id=1, replica_groups=mesh['ctx'=4,'ep'=8] {'ctx'}, dimensions={0}, use_global_device_ids=true | all-gather | bytes 737280 | tf_op jit(solution)/shard_map/all_gather | solution.py:37
  12.0 2.8 %fusion.23 = f32[512,128,16]{1,0,2:T(8,128)S(1)} fusion(bf16[128,16,512]{2,1,0:T(8,128)(2,1)S(1)} %bitcast.145, bf16[512,576]{1,0:T(8,128)(2,1)S(1)} %all_gather.3), kind=kOutput, calls=%fused_computation.27 | convolution fusion | flops 1073741824 | bytes 6815744 | tf_op jit(solution)/shard_map/sthd,sjd->shtj/dot_general | solution.py:44
  16.3 4.1 %bitcast_convert_fusion = (f32[16,128,512]{1,2,0:T(8,128)}, bf16[512,16,128]{2,0,1:T(8,128)(2,1)}) fusion(f32[16,128]{1,0:T(8,128)S(1)} %fusion.5, f32[1,16,128,512]{2,3,1,0:T(8,128)S(1)} %get-tuple-element.31, f32[16,128]{1,0:T(8,128)S(1)} %get-tuple-element.30, bf16[512,576]{1,0:T(8,128)(2,1)S(1)} %all_gather.3), kind=kOutput, calls=%fused_computation.18 | convolution fusion | flops 1078984704 | bytes 11026432 | tf_op jit(solution)/shard_map/shtj,sjd->sthd/dot_general | solution.py:55
  20.4 5.5 %copy.52 = f32[16,128,512]{2,0,1:T(8,128)} copy(f32[16,128,512]{1,2,0:T(8,128)} %get-tuple-element.32) | data formatting | bytes 8388608
  25.9 3.3 %multiply_reduce_fusion = f32[16,128]{0,1:T(8,128)S(1)} fusion(f32[16,128,512]{2,0,1:T(8,128)} %copy.52, bf16[1,128,16,512]{3,2,1,0:T(8,128)(2,1)} %param.11), kind=kLoop, calls=%fused_computation.6 | loop fusion | flops 3143680 | bytes 6299648
  29.3 6.8 %fusion.28 = f32[512,512]{1,0:T(8,128)} fusion(bf16[128,16,512]{2,1,0:T(8,128)(2,1)} %bitcast.147, f32[16,128]{1,0:T(8,128)S(1)} %fusion.5, f32[1,16,128,512]{2,3,1,0:T(8,128)} %copy-done.1, f32[16,128]{1,0:T(8,128)S(1)} %get-tuple-element.30), kind=kOutput, calls=%fused_computation.30 | convolution fusion | flops 1076887552 | bytes 7356416 | tf_op jit(solution)/shard_map/shtj,sthd->jd/dot_general | solution.py:76
  36.1 4.7 %fusion.1 = bf16[1,16,128,512]{2,3,1,0:T(8,128)(2,1)} fusion(f32[16,128]{1,0:T(8,128)S(1)} %copy.53, bf16[128,16,512]{2,1,0:T(8,128)(2,1)S(1)} %bitcast.148, f32[16,128]{1,0:T(8,128)S(1)} %fusion.5, f32[1,16,128,512]{2,3,1,0:T(8,128)S(1)} %copy-done.2, f32[16,128]{1,0:T(8,128)S(1)} %get-tuple-element.30, bf16[512,576]{1,0:T(8,128)(2,1)S(1)} %all_gather.3), kind=kOutput, calls=%fused_computation.2 | convolution fusion | flops 1078984704 | bytes 8937472 | tf_op jit(solution)/shard_map/sthd,sjd->shtj/dot_general | solution.py:61
  40.8 2.3 %fusion.69 = bf16[512,64]{0,1:T(8,128)(2,1)S(1)} fusion(bf16[1,16,128,512]{2,3,1,0:T(8,128)(2,1)} %fusion.1, bf16[1,16,64,128]{3,2,1,0:T(8,128)(2,1)S(1)} %copy-done.4), kind=kOutput, calls=%fused_computation.45 | convolution fusion | flops 134283264 | bytes 2424832 | tf_op jit(solution)/shard_map/shtj,shdt->jd/dot_general | solution.py:79
  43.2 4.4 %fusion.48 = bf16[512,512]{1,0:T(8,128)(2,1)S(1)} fusion(f32[512,512]{1,0:T(8,128)} %fusion.28, bf16[128,16,512]{2,1,0:T(8,128)(2,1)S(1)} %bitcast.146, bf16[1,16,128,512]{2,3,1,0:T(8,128)(2,1)} %fusion.1), kind=kOutput, calls=%fused_computation.34 | convolution fusion | flops 1074528256 | bytes 5767168 | tf_op jit(solution)/shard_map/shtj,sthd->jd/dot_general | solution.py:73
  48.6 1.3 %collective-permute-start.2 = (bf16[128,576]{1,0:T(8,128)(2,1)}, bf16[128,576]{1,0:T(8,128)(2,1)}, u32[]{:S(2)}, u32[]{:S(2)}) collective-permute-start(bf16[128,576]{1,0:T(8,128)(2,1)} %get-tuple-element.29), channel_id=1, source_target_pairs={{24,0},{25,1},{26,2},{27,3},{28,4},{29,5},{30,6},{31,7}} | collective-permute-start | bytes 442376 | tf_op jit(solution)/shard_map/ppermute | solution.py:14
  49.9 1.3 %collective-permute-start.1 = (bf16[128,576]{1,0:T(8,128)(2,1)}, bf16[128,576]{1,0:T(8,128)(2,1)}, u32[]{:S(2)}, u32[]{:S(2)}) collective-permute-start(bf16[128,576]{1,0:T(8,128)(2,1)} %get-tuple-element.28), channel_id=1, source_target_pairs={{16,0},{24,8},{17,1},{25,9},{18,2},{26,10},{19,3},{27,11},{20,4},{... | collective-permute-start | bytes 442376 | tf_op jit(solution)/shard_map/ppermute | solution.py:14
  51.2 1.3 %collective-permute-start = (bf16[128,576]{1,0:T(8,128)(2,1)}, bf16[128,576]{1,0:T(8,128)(2,1)}, u32[]{:S(2)}, u32[]{:S(2)}) collective-permute-start(bf16[128,576]{1,0:T(8,128)(2,1)} %get-tuple-element.27), channel_id=1, source_target_pairs={{8,0},{16,8},{24,16},{9,1},{17,9},{25,17},{10,2},{18,10},{26,18},{... | collective-permute-start | bytes 442376 | tf_op jit(solution)/shard_map/ppermute | solution.py:14
  52.5 3.0 %collective-permute-done.2 = bf16[128,576]{1,0:T(8,128)(2,1)} collective-permute-done((bf16[128,576]{1,0:T(8,128)(2,1)}, bf16[128,576]{1,0:T(8,128)(2,1)}, u32[]{:S(2)}, u32[]{:S(2)}) %collective-permute-start.2) | collective-permute-done | bytes 147488 | tf_op jit(solution)/shard_map/ppermute | solution.py:14
  55.5 3.6 %collective-permute-done.1 = bf16[128,576]{1,0:T(8,128)(2,1)} collective-permute-done((bf16[128,576]{1,0:T(8,128)(2,1)}, bf16[128,576]{1,0:T(8,128)(2,1)}, u32[]{:S(2)}, u32[]{:S(2)}) %collective-permute-start.1) | collective-permute-done | bytes 147488 | tf_op jit(solution)/shard_map/ppermute | solution.py:14
  59.1 1.2 %add_convert_fusion.3 = bf16[128,576]{1,0:T(8,128)(2,1)S(1)} fusion(bf16[128,576]{1,0:T(8,128)(2,1)} %collective-permute-done.2, bf16[128,576]{1,0:T(8,128)(2,1)} %collective-permute-done.1, bf16[128,576]{1,0:T(8,128)(2,1)} %collective-permute-done, s32[]{:T(128)S(6)} %select_n.22, bf16[4,128,512]{2,1,0:T(8,128)(2,1)S(1)} %bitcast.151, ...), kind=kLoop, calls=%fused_computation.54 | loop fusion | flops 958464 | bytes 1179653 | tf_op jit(solution)/shard_map/convert_element_type | solution.py:24
  60.3 1.6 %collective-permute-start.3 = (bf16[128,576]{1,0:T(8,128)(2,1)S(1)}, bf16[128,576]{1,0:T(8,128)(2,1)S(1)}, u32[]{:S(2)}, u32[]{:S(2)}) collective-permute-start(bf16[128,576]{1,0:T(8,128)(2,1)S(1)} %add_convert_fusion.3), channel_id=1, source_target_pairs={{0,1},{1,0},{2,3},{3,2},{4,5},{5,4},{6,7},{7,6},{8,9},{9,8},{10,11... | collective-permute-start | bytes 442376 | tf_op jit(solution)/shard_map/ppermute | solution.py:25
  61.9 4.9 %collective-permute-done.3 = bf16[128,576]{1,0:T(8,128)(2,1)S(1)} collective-permute-done((bf16[128,576]{1,0:T(8,128)(2,1)S(1)}, bf16[128,576]{1,0:T(8,128)(2,1)S(1)}, u32[]{:S(2)}, u32[]{:S(2)}) %collective-permute-start.3) | collective-permute-done | bytes 147488 | tf_op jit(solution)/shard_map/ppermute | solution.py:25
  66.8 1.6 %collective-permute-start.4 = (bf16[128,576]{1,0:T(8,128)(2,1)S(1)}, bf16[128,576]{1,0:T(8,128)(2,1)S(1)}, u32[]{:S(2)}, u32[]{:S(2)}) collective-permute-start(bf16[128,576]{1,0:T(8,128)(2,1)S(1)} %add_convert_fusion.2), channel_id=1, source_target_pairs={{0,2},{1,3},{2,0},{3,1},{4,6},{5,7},{6,4},{7,5},{8,10},{9,11},{10,... | collective-permute-start | bytes 442376 | tf_op jit(solution)/shard_map/ppermute | solution.py:25
  68.5 4.2 %fusion.25 = bf16[1,128,16,512]{1,3,2,0:T(8,128)(2,1)} fusion(bf16[1,16,128,512]{2,3,1,0:T(8,128)(2,1)} %fusion.1, bf16[512,576]{1,0:T(8,128)(2,1)S(1)} %all_gather.3), kind=kOutput, calls=%fused_computation.29 | convolution fusion | flops 1075838976 | bytes 4718592 | tf_op jit(solution)/shard_map/shtj,sjd->sthd/dot_general | solution.py:67
  72.7 4.5 %copy.41 = bf16[1,128,16,512]{3,2,1,0:T(8,128)(2,1)} copy(bf16[1,128,16,512]{1,3,2,0:T(8,128)(2,1)} %bitcast.149) | data formatting | bytes 4194304
  77.2 4.5 %copy.42 = bf16[1,128,16,512]{3,2,1,0:T(8,128)(2,1)} copy(bf16[1,128,16,512]{1,3,2,0:T(8,128)(2,1)} %fusion.25) | data formatting | bytes 4194304
  81.7 2.6 %collective-permute-start.5 = (bf16[128,576]{1,0:T(8,128)(2,1)S(1)}, bf16[128,576]{1,0:T(8,128)(2,1)S(1)}, u32[]{:S(2)}, u32[]{:S(2)}) collective-permute-start(bf16[128,576]{1,0:T(8,128)(2,1)S(1)} %add_convert_fusion.1), channel_id=1, source_target_pairs={{0,4},{1,5},{2,6},{3,7},{4,0},{5,1},{6,2},{7,3},{8,12},{9,13},{10,... | collective-permute-start | bytes 442376 | tf_op jit(solution)/shard_map/ppermute | solution.py:25
  84.3 2.8 %fusion.60 = bf16[1,16,64,128]{3,2,1,0:T(8,128)(2,1)} fusion(bf16[1,16,128,512]{2,3,1,0:T(8,128)(2,1)} %fusion.1, bf16[512,576]{1,0:T(8,128)(2,1)S(1)} %all_gather.3), kind=kOutput, calls=%fused_computation.42 | convolution fusion | flops 134479872 | bytes 2490368 | tf_op jit(solution)/shard_map/shtj,sdj->shdt/dot_general | solution.py:71
  87.1 5.2 %collective-permute-done.5 = bf16[128,576]{1,0:T(8,128)(2,1)S(1)} collective-permute-done((bf16[128,576]{1,0:T(8,128)(2,1)S(1)}, bf16[128,576]{1,0:T(8,128)(2,1)S(1)}, u32[]{:S(2)}, u32[]{:S(2)}) %collective-permute-start.5) | collective-permute-done | bytes 147488 | tf_op jit(solution)/shard_map/ppermute | solution.py:25
  (27 shorter events, 6.0 us)
Async XLA Ops:
  0.6 11.3 %copy-start = (bf16[1,128,16,512]{3,2,1,0:T(8,128)(2,1)S(1)}, bf16[1,128,16,512]{3,2,1,0:T(8,128)(2,1)}, u32[]{:S(2)}) copy-start(bf16[1,128,16,512]{3,2,1,0:T(8,128)(2,1)} %param.7) | copy-start | bytes 6291460
  12.0 2.8 %copy-start.4 = (bf16[1,16,64,128]{3,2,1,0:T(8,128)(2,1)S(1)}, bf16[1,16,64,128]{3,2,1,0:T(8,128)(2,1)}, u32[]{:S(2)}) copy-start(bf16[1,16,64,128]{3,2,1,0:T(8,128)(2,1)} %param.8) | copy-start | bytes 786436
  15.7 4.7 %copy-start.1 = (f32[1,16,128,512]{2,3,1,0:T(8,128)}, f32[1,16,128,512]{2,3,1,0:T(8,128)S(1)}, u32[]{:S(2)}) copy-start(f32[1,16,128,512]{2,3,1,0:T(8,128)S(1)} %get-tuple-element.31) | copy-start | bytes 12582916
  29.3 6.8 %copy-start.2 = (f32[1,16,128,512]{2,3,1,0:T(8,128)S(1)}, f32[1,16,128,512]{2,3,1,0:T(8,128)}, u32[]{:S(2)}) copy-start(f32[1,16,128,512]{2,3,1,0:T(8,128)} %copy-done.1) | copy-start | bytes 12582916
  29.3 6.8 %copy-start.3 = (bf16[1,128,16,512]{3,2,1,0:T(8,128)(2,1)S(1)}, bf16[1,128,16,512]{3,2,1,0:T(8,128)(2,1)}, u32[]{:S(2)}) copy-start(bf16[1,128,16,512]{3,2,1,0:T(8,128)(2,1)} %param.11) | copy-start | bytes 6291460
  48.6 6.9 %collective-permute-start.2 = (bf16[128,576]{1,0:T(8,128)(2,1)}, bf16[128,576]{1,0:T(8,128)(2,1)}, u32[]{:S(2)}, u32[]{:S(2)}) collective-permute-start(bf16[128,576]{1,0:T(8,128)(2,1)} %get-tuple-element.29), channel_id=1, source_target_pairs={{24,0},{25,1},{26,2},{27,3},{28,4},{29,5},{30,6},{31,7}} | collective-permute-start | bytes 442376 | tf_op jit(solution)/shard_map/ppermute | solution.py:14
  49.9 9.2 %collective-permute-start.1 = (bf16[128,576]{1,0:T(8,128)(2,1)}, bf16[128,576]{1,0:T(8,128)(2,1)}, u32[]{:S(2)}, u32[]{:S(2)}) collective-permute-start(bf16[128,576]{1,0:T(8,128)(2,1)} %get-tuple-element.28), channel_id=1, source_target_pairs={{16,0},{24,8},{17,1},{25,9},{18,2},{26,10},{19,3},{27,11},{20,4},{... | collective-permute-start | bytes 442376 | tf_op jit(solution)/shard_map/ppermute | solution.py:14
  51.2 7.9 %collective-permute-start = (bf16[128,576]{1,0:T(8,128)(2,1)}, bf16[128,576]{1,0:T(8,128)(2,1)}, u32[]{:S(2)}, u32[]{:S(2)}) collective-permute-start(bf16[128,576]{1,0:T(8,128)(2,1)} %get-tuple-element.27), channel_id=1, source_target_pairs={{8,0},{16,8},{24,16},{9,1},{17,9},{25,17},{10,2},{18,10},{26,18},{... | collective-permute-start | bytes 442376 | tf_op jit(solution)/shard_map/ppermute | solution.py:14
  60.3 6.5 %collective-permute-start.3 = (bf16[128,576]{1,0:T(8,128)(2,1)S(1)}, bf16[128,576]{1,0:T(8,128)(2,1)S(1)}, u32[]{:S(2)}, u32[]{:S(2)}) collective-permute-start(bf16[128,576]{1,0:T(8,128)(2,1)S(1)} %add_convert_fusion.3), channel_id=1, source_target_pairs={{0,1},{1,0},{2,3},{3,2},{4,5},{5,4},{6,7},{7,6},{8,9},{9,8},{10,11... | collective-permute-start | bytes 442376 | tf_op jit(solution)/shard_map/ppermute | solution.py:25
  66.8 14.8 %collective-permute-start.4 = (bf16[128,576]{1,0:T(8,128)(2,1)S(1)}, bf16[128,576]{1,0:T(8,128)(2,1)S(1)}, u32[]{:S(2)}, u32[]{:S(2)}) collective-permute-start(bf16[128,576]{1,0:T(8,128)(2,1)S(1)} %add_convert_fusion.2), channel_id=1, source_target_pairs={{0,2},{1,3},{2,0},{3,1},{4,6},{5,7},{6,4},{7,5},{8,10},{9,11},{10,... | collective-permute-start | bytes 442376 | tf_op jit(solution)/shard_map/ppermute | solution.py:25
  81.7 10.6 %collective-permute-start.5 = (bf16[128,576]{1,0:T(8,128)(2,1)S(1)}, bf16[128,576]{1,0:T(8,128)(2,1)S(1)}, u32[]{:S(2)}, u32[]{:S(2)}) collective-permute-start(bf16[128,576]{1,0:T(8,128)(2,1)S(1)} %add_convert_fusion.1), channel_id=1, source_target_pairs={{0,4},{1,5},{2,6},{3,7},{4,0},{5,1},{6,2},{7,3},{8,12},{9,13},{10,... | collective-permute-start | bytes 442376 | tf_op jit(solution)/shard_map/ppermute | solution.py:25
where the time goes:
time: 94.3 us; the launch traced here: 93.7 us
  matrix products  33.1 us (35%)
  local copies, waits for them, and re-layouts  17 us (18%)
  waiting for transfers between devices  16.8 us (18%)
  starting transfers between devices  9.74 us (10%)
  blocking collectives  9.33 us (10%)
  other arithmetic  7.04 us (7%)
    unnamed x15, local copies, waits for them, and re-layouts  16.2 us
    ppermute x3, waiting for transfers between devices, butterfly_sum_ep(): theirs = lax.ppermute(mine, 'ep', [(i, i ^ bit) for i in range(n_ep)])  10.1 us
    all_gather x1, blocking collectives, body(): whole_keys = lax.all_gather(local_keys, 'ctx', axis=0, tiled=True)  9.33 us
    dot_general x1, matrix products, body(): jnp.einsum('shtj,sthd->jd', rounded_weights, output_grad, preferred_eleme...  6.77 us
    ppermute x3, waiting for transfers between devices, causal_reduce_ctx(): lax.ppermute(sent, 'ctx', [(i, i - shift) for i in range(shift, n_ctx)])  6.64 us
    ppermute x3, starting transfers between devices, butterfly_sum_ep(): theirs = lax.ppermute(mine, 'ep', [(i, i ^ bit) for i in range(n_ep)])  5.87 us
    dot_general x1, matrix products, body(): jnp.einsum('sthd,sjd->shtj', output_grad, whole_latent, preferred_element...  4.71 us
    dot_general x1, matrix products, body(): jnp.einsum('shtj,sthd->jd', score_grad, query_latent, preferred_element_t...  4.44 us
  transfers between devices with their start and end apart: 6, of which 4 were waited for; matrix products, arithmetic and copies ran while one was open for 17% of the time, Pallas kernels for 0%

commit v1 on v0

--- a/solution.py
+++ b/solution.py
@@ -4,6 +4,35 @@
 from jax.sharding import PartitionSpec as P
 
 scale_factor = 192.0 ** (-0.5)
+
+
+def cut_members_all_on(packet, along_axis):
+    carry = lax.axis_size(along_axis)
+    f_now, state_next, local_next = (carry, lax.axis_index(along_axis), packet.shape[0])
+    all_blocks = [rr * f_now if p == 0 else rr for p, rr in enumerate(packet.shape)]
+    found_now = lax.dynamic_update_slice_in_dim(
+        jnp.zeros(all_blocks, packet.dtype), packet, state_next * local_next, axis=0
+    )
+    f_next = kept_arr = packet
+    for src_i in range(1, f_now // 2 + 1):
+        f_next = lax.ppermute(
+            f_next,
+            axis_name=along_axis,
+            perm=list(map(lambda p: (p, (p + 1) % f_now), range(f_now))),
+        )
+        found_now = lax.dynamic_update_slice_in_dim(
+            found_now, f_next, (state_next - src_i) % f_now * local_next, axis=0
+        )
+        if 2 * src_i < f_now:
+            kept_arr = lax.ppermute(
+                kept_arr,
+                axis_name=along_axis,
+                perm=list(map(lambda p: (p, (p - 1) % f_now), range(f_now))),
+            )
+            found_now = lax.dynamic_update_slice_in_dim(
+                found_now, kept_arr, (state_next + src_i) % f_now * local_next, axis=0
+            )
+    return found_now
 
 
 def causal_reduce_ctx(blocks, n_ctx):
@@ -34,7 +63,7 @@
     block_len = query_latent.shape[1]
     kvr = key_latent.shape[2]
     local_keys = jnp.concatenate([key_latent[0], key_rope[0].T], axis=1)
-    whole_keys = lax.all_gather(local_keys, "ctx", axis=0, tiled=True)
+    whole_keys = cut_members_all_on(local_keys, "ctx")
     whole_latent = whole_keys[None, :, :kvr]
     whole_rope = whole_keys[:, kvr:].T[None]
     length = whole_latent.shape[1]

time: 94.3 us -> 90.7 us (0.962)
  blocking collectives: 9.33 us -> 0 us
  waiting for transfers between devices: 16.8 us -> 23.4 us
  matrix products: 33.1 us -> 27.3 us
  starting transfers between devices: 9.74 us -> 13.9 us
    all_gather x1 -> x0, blocking collectives: 9.33 us -> none  [body(): whole_keys = lax.all_gather(local_keys, 'ctx', axis=0, tiled=True)]
    ppermute x0 -> x3, waiting for transfers between devices: none -> 5.89 us  [the longest x2 5.89 us: cut_members_all_on(): lax.ppermute(f_next, axis_name=along_axis, perm=list(map(lambda p: (p, (p...]
    ppermute x0 -> x3, starting transfers between devices: none -> 4.1 us  [the longest x2 2.11 us: cut_members_all_on(): lax.ppermute(f_next, axis_name=along_axis, perm=list(map(lambda p: (p, (p...]
    dot_general x1, matrix products: 4.44 us -> 2.57 us  [body(): jnp.einsum('shtj,sthd->jd', score_grad, query_latent, preferred_element_t...]
    dot_general x1, matrix products: 2.34 us -> 0.75 us  [body(): jnp.einsum('shtj,shdt->jd', score_grad, query_rope, preferred_element_typ...]
    dot_general x1, matrix products: 4.71 us -> 3.37 us  [body(): jnp.einsum('sthd,sjd->shtj', output_grad, whole_latent, preferred_element...]
    dot_general x1, matrix products: 6.77 us -> 5.8 us  [body(): jnp.einsum('shtj,sthd->jd', rounded_weights, output_grad, preferred_eleme...]
    unnamed x15 -> x17, local copies, waits for them, and re-layouts: 16.2 us -> 16.8 us
  transfers between devices with their start and end apart: 6 -> 9, of which waited for: 4 -> 6; matrix products, arithmetic and copies ran while one was open for 17% -> 18% of each run, Pallas kernels for 0% -> 0%
where the time goes in v1:
time: 90.7 us; the launch traced here: 90.2 us
  matrix products  27.3 us (30%)
  waiting for transfers between devices  23.4 us (26%)
  local copies, waits for them, and re-layouts  17.7 us (20%)
  starting transfers between devices  13.9 us (15%)
  other arithmetic  7.05 us (8%)
    unnamed x17, local copies, waits for them, and re-layouts  16.8 us
    ppermute x3, waiting for transfers between devices, butterfly_sum_ep(): theirs = lax.ppermute(mine, 'ep', [(i, i ^ bit) for i in range(n_ep)])  10.1 us
    ppermute x3, waiting for transfers between devices, causal_reduce_ctx(): lax.ppermute(sent, 'ctx', [(i, i - shift) for i in range(shift, n_ctx)])  7.35 us
    ppermute x3, starting transfers between devices, butterfly_sum_ep(): theirs = lax.ppermute(mine, 'ep', [(i, i ^ bit) for i in range(n_ep)])  5.9 us
    ppermute x2, waiting for transfers between devices, cut_members_all_on(): lax.ppermute(f_next, axis_name=along_axis, perm=list(map(lambda p: (p, (p...  5.89 us
    dot_general x1, matrix products, body(): jnp.einsum('shtj,sthd->jd', rounded_weights, output_grad, preferred_eleme...  5.8 us
    dot_general x1, matrix products, body(): jnp.einsum('shtj,sjd->sthd', score_grad, whole_latent, preferred_element_...  4.19 us
    dot_general x1, matrix products, body(): jnp.einsum('shtj,sjd->sthd', rounded_weights, whole_latent, preferred_ele...  4.12 us
  transfers between devices with their start and end apart: 9, of which 6 were waited for; matrix products, arithmetic and copies ran while one was open for 18% of the time, Pallas kernels for 0%

profile of v1, /device:TPU:0, one launch (start us, length us, event | category | flops | bytes accessed | tf_op | source)
XLA Modules:
  0.0 90.2 jit_solution(563572583066952554)
XLA Ops:
  3.1 2.0 %collective-permute-start.1 = (bf16[128,576]{1,0:T(8,128)(2,1)S(1)}, bf16[128,576]{1,0:T(8,128)(2,1)S(1)}, u32[]{:S(2)}, u32[]{:S(2)}) collective-permute-start(bf16[128,576]{1,0:T(8,128)(2,1)S(1)} %get-tuple-element.30), channel_id=1, source_target_pairs={{0,24},{8,0},{16,8},{24,16},{1,25},{9,1},{17,9},{25,17},{2,26},{10... | collective-permute-start | bytes 442376 | tf_op jit(solution)/shard_map/ppermute | solution.py:27
  5.3 2.8 %collective-permute-done = bf16[128,576]{1,0:T(8,128)(2,1)S(1)} collective-permute-done((bf16[128,576]{1,0:T(8,128)(2,1)S(1)}, bf16[128,576]{1,0:T(8,128)(2,1)S(1)}, u32[]{:S(2)}, u32[]{:S(2)}) %collective-permute-start) | collective-permute-done | bytes 147488 | tf_op jit(solution)/shard_map/ppermute | solution.py:18
  8.1 1.6 %collective-permute-start.2 = (bf16[128,576]{1,0:T(8,128)(2,1)S(1)}, bf16[128,576]{1,0:T(8,128)(2,1)S(1)}, u32[]{:S(2)}, u32[]{:S(2)}) collective-permute-start(bf16[128,576]{1,0:T(8,128)(2,1)S(1)} %collective-permute-done), channel_id=1, source_target_pairs={{0,8},{8,16},{16,24},{24,0},{1,9},{9,17},{17,25},{25,1},{2,10},{10... | collective-permute-start | bytes 442376 | tf_op jit(solution)/shard_map/ppermute | solution.py:18
  9.8 3.1 %collective-permute-done.2 = bf16[128,576]{1,0:T(8,128)(2,1)S(1)} collective-permute-done((bf16[128,576]{1,0:T(8,128)(2,1)S(1)}, bf16[128,576]{1,0:T(8,128)(2,1)S(1)}, u32[]{:S(2)}, u32[]{:S(2)}) %collective-permute-start.2) | collective-permute-done | bytes 147488 | tf_op jit(solution)/shard_map/ppermute | solution.py:18
  12.9 2.8 %fusion.23 = f32[512,128,16]{1,0,2:T(8,128)S(1)} fusion(bf16[128,16,512]{2,1,0:T(8,128)(2,1)S(1)} %bitcast.145, bf16[512,576]{1,0:T(8,128)(2,1)S(1)} %constant_dynamic-update-slice_fusion), kind=kOutput, calls=%fused_computation.27 | convolution fusion | flops 1073741824 | bytes 6815744 | tf_op jit(solution)/shard_map/sthd,sjd->shtj/dot_general | solution.py:73
  17.2 4.1 %bitcast_convert_fusion = (f32[16,128,512]{1,2,0:T(8,128)}, bf16[512,16,128]{2,0,1:T(8,128)(2,1)}) fusion(f32[16,128]{1,0:T(8,128)S(1)} %fusion.5, f32[1,16,128,512]{2,3,1,0:T(8,128)S(1)} %get-tuple-element.33, f32[16,128]{1,0:T(8,128)S(1)} %get-tuple-element.32, bf16[512,576]{1,0:T(8,128)(2,1)S(1)} %constant_dynamic-update-slice_fusion), kind=kOutput, calls=%fused_computation.18 | convolution fusion | flops 1078984704 | bytes 11026432 | tf_op jit(solution)/shard_map/shtj,sjd->sthd/dot_general | solution.py:84
  21.3 5.5 %copy.52 = f32[16,128,512]{2,0,1:T(8,128)} copy(f32[16,128,512]{1,2,0:T(8,128)} %get-tuple-element.34) | data formatting | bytes 8388608
  26.8 3.3 %multiply_reduce_fusion = f32[16,128]{0,1:T(8,128)S(1)} fusion(f32[16,128,512]{2,0,1:T(8,128)} %copy.52, bf16[1,128,16,512]{3,2,1,0:T(8,128)(2,1)} %param.11), kind=kLoop, calls=%fused_computation.6 | loop fusion | flops 3143680 | bytes 6299648
  30.2 5.8 %fusion.28 = f32[512,512]{1,0:T(8,128)S(1)} fusion(bf16[128,16,512]{2,1,0:T(8,128)(2,1)} %bitcast.147, f32[16,128]{1,0:T(8,128)S(1)} %fusion.5, f32[1,16,128,512]{2,3,1,0:T(8,128)} %copy-done.1, f32[16,128]{1,0:T(8,128)S(1)} %get-tuple-element.32), kind=kOutput, calls=%fused_computation.30 | convolution fusion | flops 1076887552 | bytes 7356416 | tf_op jit(solution)/shard_map/shtj,sthd->jd/dot_general | solution.py:105
  36.0 3.4 %fusion.1 = bf16[1,16,128,512]{2,3,1,0:T(8,128)(2,1)S(1)} fusion(f32[16,128]{1,0:T(8,128)S(1)} %copy.53, bf16[128,16,512]{2,1,0:T(8,128)(2,1)S(1)} %bitcast.148, f32[16,128]{1,0:T(8,128)S(1)} %fusion.5, f32[1,16,128,512]{2,3,1,0:T(8,128)S(1)} %copy-done.2, f32[16,128]{1,0:T(8,128)S(1)} %get-tuple-element.32, ...), kind=kOutput, calls=%fused_computation.2 | convolution fusion | flops 1078984704 | bytes 8937472 | tf_op jit(solution)/shard_map/sthd,sjd->shtj/dot_general | solution.py:90
  40.8 2.6 %fusion.48 = bf16[512,512]{1,0:T(8,128)(2,1)S(1)} fusion(f32[512,512]{1,0:T(8,128)S(1)} %fusion.28, bf16[128,16,512]{2,1,0:T(8,128)(2,1)S(1)} %bitcast.146, bf16[1,16,128,512]{2,3,1,0:T(8,128)(2,1)S(1)} %fusion.1), kind=kOutput, calls=%fused_computation.34 | convolution fusion | flops 1074528256 | bytes 5767168 | tf_op jit(solution)/shard_map/shtj,sthd->jd/dot_general | solution.py:102
  45.6 1.3 %collective-permute-start.4 = (bf16[128,576]{1,0:T(8,128)(2,1)}, bf16[128,576]{1,0:T(8,128)(2,1)}, u32[]{:S(2)}, u32[]{:S(2)}) collective-permute-start(bf16[128,576]{1,0:T(8,128)(2,1)} %get-tuple-element.28), channel_id=1, source_target_pairs={{16,0},{24,8},{17,1},{25,9},{18,2},{26,10},{19,3},{27,11},{20,4},{... | collective-permute-start | bytes 442376 | tf_op jit(solution)/shard_map/ppermute | solution.py:43
  46.9 1.3 %collective-permute-start.3 = (bf16[128,576]{1,0:T(8,128)(2,1)}, bf16[128,576]{1,0:T(8,128)(2,1)}, u32[]{:S(2)}, u32[]{:S(2)}) collective-permute-start(bf16[128,576]{1,0:T(8,128)(2,1)} %get-tuple-element.27), channel_id=1, source_target_pairs={{8,0},{16,8},{24,16},{9,1},{17,9},{25,17},{10,2},{18,10},{26,18},{... | collective-permute-start | bytes 442376 | tf_op jit(solution)/shard_map/ppermute | solution.py:43
  48.2 3.0 %collective-permute-done.5 = bf16[128,576]{1,0:T(8,128)(2,1)} collective-permute-done((bf16[128,576]{1,0:T(8,128)(2,1)}, bf16[128,576]{1,0:T(8,128)(2,1)}, u32[]{:S(2)}, u32[]{:S(2)}) %collective-permute-start.5) | collective-permute-done | bytes 147488 | tf_op jit(solution)/shard_map/ppermute | solution.py:43
  51.2 4.3 %collective-permute-done.4 = bf16[128,576]{1,0:T(8,128)(2,1)} collective-permute-done((bf16[128,576]{1,0:T(8,128)(2,1)}, bf16[128,576]{1,0:T(8,128)(2,1)}, u32[]{:S(2)}, u32[]{:S(2)}) %collective-permute-start.4) | collective-permute-done | bytes 147488 | tf_op jit(solution)/shard_map/ppermute | solution.py:43
  56.7 1.6 %collective-permute-start.6 = (bf16[128,576]{1,0:T(8,128)(2,1)S(1)}, bf16[128,576]{1,0:T(8,128)(2,1)S(1)}, u32[]{:S(2)}, u32[]{:S(2)}) collective-permute-start(bf16[128,576]{1,0:T(8,128)(2,1)S(1)} %add_convert_fusion.3), channel_id=1, source_target_pairs={{0,1},{1,0},{2,3},{3,2},{4,5},{5,4},{6,7},{7,6},{8,9},{9,8},{10,11... | collective-permute-start | bytes 442376 | tf_op jit(solution)/shard_map/ppermute | solution.py:54
  58.3 5.0 %collective-permute-done.6 = bf16[128,576]{1,0:T(8,128)(2,1)S(1)} collective-permute-done((bf16[128,576]{1,0:T(8,128)(2,1)S(1)}, bf16[128,576]{1,0:T(8,128)(2,1)S(1)}, u32[]{:S(2)}, u32[]{:S(2)}) %collective-permute-start.6) | collective-permute-done | bytes 147488 | tf_op jit(solution)/shard_map/ppermute | solution.py:54
  63.3 1.6 %collective-permute-start.7 = (bf16[128,576]{1,0:T(8,128)(2,1)S(1)}, bf16[128,576]{1,0:T(8,128)(2,1)S(1)}, u32[]{:S(2)}, u32[]{:S(2)}) collective-permute-start(bf16[128,576]{1,0:T(8,128)(2,1)S(1)} %add_convert_fusion.2), channel_id=1, source_target_pairs={{0,2},{1,3},{2,0},{3,1},{4,6},{5,7},{6,4},{7,5},{8,10},{9,11},{10,... | collective-permute-start | bytes 442376 | tf_op jit(solution)/shard_map/ppermute | solution.py:54
  64.9 4.2 %fusion.25 = bf16[1,128,16,512]{1,3,2,0:T(8,128)(2,1)} fusion(bf16[1,16,128,512]{2,3,1,0:T(8,128)(2,1)} %copy-done.3, bf16[512,576]{1,0:T(8,128)(2,1)S(1)} %constant_dynamic-update-slice_fusion), kind=kOutput, calls=%fused_computation.29 | convolution fusion | flops 1075838976 | bytes 4718592 | tf_op jit(solution)/shard_map/shtj,sjd->sthd/dot_general | solution.py:96
  69.1 4.5 %copy.41 = bf16[1,128,16,512]{3,2,1,0:T(8,128)(2,1)} copy(bf16[1,128,16,512]{1,3,2,0:T(8,128)(2,1)} %bitcast.149) | data formatting | bytes 4194304
  73.6 4.5 %copy.42 = bf16[1,128,16,512]{3,2,1,0:T(8,128)(2,1)} copy(bf16[1,128,16,512]{1,3,2,0:T(8,128)(2,1)} %fusion.25) | data formatting | bytes 4194304
  78.2 2.7 %collective-permute-start.8 = (bf16[128,576]{1,0:T(8,128)(2,1)S(1)}, bf16[128,576]{1,0:T(8,128)(2,1)S(1)}, u32[]{:S(2)}, u32[]{:S(2)}) collective-permute-start(bf16[128,576]{1,0:T(8,128)(2,1)S(1)} %add_convert_fusion.1), channel_id=1, source_target_pairs={{0,4},{1,5},{2,6},{3,7},{4,0},{5,1},{6,2},{7,3},{8,12},{9,13},{10,... | collective-permute-start | bytes 442376 | tf_op jit(solution)/shard_map/ppermute | solution.py:54
  80.8 2.8 %fusion.60 = bf16[1,16,64,128]{3,2,1,0:T(8,128)(2,1)} fusion(bf16[1,16,128,512]{2,3,1,0:T(8,128)(2,1)} %copy-done.3, bf16[512,576]{1,0:T(8,128)(2,1)S(1)} %constant_dynamic-update-slice_fusion), kind=kOutput, calls=%fused_computation.42 | convolution fusion | flops 134479872 | bytes 2490368 | tf_op jit(solution)/shard_map/shtj,sdj->shdt/dot_general | solution.py:100
  83.6 5.2 %collective-permute-done.8 = bf16[128,576]{1,0:T(8,128)(2,1)S(1)} collective-permute-done((bf16[128,576]{1,0:T(8,128)(2,1)S(1)}, bf16[128,576]{1,0:T(8,128)(2,1)S(1)}, u32[]{:S(2)}, u32[]{:S(2)}) %collective-permute-start.8) | collective-permute-done | bytes 147488 | tf_op jit(solution)/shard_map/ppermute | solution.py:54
  (38 shorter events, 10.4 us)
Async XLA Ops:
  0.6 12.2 %copy-start = (bf16[1,128,16,512]{3,2,1,0:T(8,128)(2,1)S(1)}, bf16[1,128,16,512]{3,2,1,0:T(8,128)(2,1)}, u32[]{:S(2)}) copy-start(bf16[1,128,16,512]{3,2,1,0:T(8,128)(2,1)} %param.7) | copy-start | bytes 6291460
  2.6 5.4 %collective-permute-start = (bf16[128,576]{1,0:T(8,128)(2,1)S(1)}, bf16[128,576]{1,0:T(8,128)(2,1)S(1)}, u32[]{:S(2)}, u32[]{:S(2)}) collective-permute-start(bf16[128,576]{1,0:T(8,128)(2,1)S(1)} %get-tuple-element.30), channel_id=1, source_target_pairs={{0,8},{8,16},{16,24},{24,0},{1,9},{9,17},{17,25},{25,1},{2,10},{10... | collective-permute-start | bytes 442376 | tf_op jit(solution)/shard_map/ppermute | solution.py:18
  3.1 6.6 %collective-permute-start.1 = (bf16[128,576]{1,0:T(8,128)(2,1)S(1)}, bf16[128,576]{1,0:T(8,128)(2,1)S(1)}, u32[]{:S(2)}, u32[]{:S(2)}) collective-permute-start(bf16[128,576]{1,0:T(8,128)(2,1)S(1)} %get-tuple-element.30), channel_id=1, source_target_pairs={{0,24},{8,0},{16,8},{24,16},{1,25},{9,1},{17,9},{25,17},{2,26},{10... | collective-permute-start | bytes 442376 | tf_op jit(solution)/shard_map/ppermute | solution.py:27
  8.1 4.7 %collective-permute-start.2 = (bf16[128,576]{1,0:T(8,128)(2,1)S(1)}, bf16[128,576]{1,0:T(8,128)(2,1)S(1)}, u32[]{:S(2)}, u32[]{:S(2)}) collective-permute-start(bf16[128,576]{1,0:T(8,128)(2,1)S(1)} %collective-permute-done), channel_id=1, source_target_pairs={{0,8},{8,16},{16,24},{24,0},{1,9},{9,17},{17,25},{25,1},{2,10},{10... | collective-permute-start | bytes 442376 | tf_op jit(solution)/shard_map/ppermute | solution.py:18
  12.9 2.8 %copy-start.5 = (bf16[1,16,64,128]{3,2,1,0:T(8,128)(2,1)S(1)}, bf16[1,16,64,128]{3,2,1,0:T(8,128)(2,1)}, u32[]{:S(2)}) copy-start(bf16[1,16,64,128]{3,2,1,0:T(8,128)(2,1)} %param.8) | copy-start | bytes 786436
  16.6 4.7 %copy-start.1 = (f32[1,16,128,512]{2,3,1,0:T(8,128)}, f32[1,16,128,512]{2,3,1,0:T(8,128)S(1)}, u32[]{:S(2)}) copy-start(f32[1,16,128,512]{2,3,1,0:T(8,128)S(1)} %get-tuple-element.33) | copy-start | bytes 12582916
  30.2 5.8 %copy-start.2 = (f32[1,16,128,512]{2,3,1,0:T(8,128)S(1)}, f32[1,16,128,512]{2,3,1,0:T(8,128)}, u32[]{:S(2)}) copy-start(f32[1,16,128,512]{2,3,1,0:T(8,128)} %copy-done.1) | copy-start | bytes 12582916
  30.2 5.8 %copy-start.4 = (bf16[1,128,16,512]{3,2,1,0:T(8,128)(2,1)S(1)}, bf16[1,128,16,512]{3,2,1,0:T(8,128)(2,1)}, u32[]{:S(2)}) copy-start(bf16[1,128,16,512]{3,2,1,0:T(8,128)(2,1)} %param.11) | copy-start | bytes 6291460
  39.4 1.3 %copy-start.3 = (bf16[1,16,128,512]{2,3,1,0:T(8,128)(2,1)}, bf16[1,16,128,512]{2,3,1,0:T(8,128)(2,1)S(1)}, u32[]{:S(2)}) copy-start(bf16[1,16,128,512]{2,3,1,0:T(8,128)(2,1)S(1)} %fusion.1) | copy-start | bytes 6291460
  44.3 6.9 %collective-permute-start.5 = (bf16[128,576]{1,0:T(8,128)(2,1)}, bf16[128,576]{1,0:T(8,128)(2,1)}, u32[]{:S(2)}, u32[]{:S(2)}) collective-permute-start(bf16[128,576]{1,0:T(8,128)(2,1)} %get-tuple-element.29), channel_id=1, source_target_pairs={{24,0},{25,1},{26,2},{27,3},{28,4},{29,5},{30,6},{31,7}} | collective-permute-start | bytes 442376 | tf_op jit(solution)/shard_map/ppermute | solution.py:43
  45.6 10.0 %collective-permute-start.4 = (bf16[128,576]{1,0:T(8,128)(2,1)}, bf16[128,576]{1,0:T(8,128)(2,1)}, u32[]{:S(2)}, u32[]{:S(2)}) collective-permute-start(bf16[128,576]{1,0:T(8,128)(2,1)} %get-tuple-element.28), channel_id=1, source_target_pairs={{16,0},{24,8},{17,1},{25,9},{18,2},{26,10},{19,3},{27,11},{20,4},{... | collective-permute-start | bytes 442376 | tf_op jit(solution)/shard_map/ppermute | solution.py:43
  46.9 8.7 %collective-permute-start.3 = (bf16[128,576]{1,0:T(8,128)(2,1)}, bf16[128,576]{1,0:T(8,128)(2,1)}, u32[]{:S(2)}, u32[]{:S(2)}) collective-permute-start(bf16[128,576]{1,0:T(8,128)(2,1)} %get-tuple-element.27), channel_id=1, source_target_pairs={{8,0},{16,8},{24,16},{9,1},{17,9},{25,17},{10,2},{18,10},{26,18},{... | collective-permute-start | bytes 442376 | tf_op jit(solution)/shard_map/ppermute | solution.py:43
  56.7 6.6 %collective-permute-start.6 = (bf16[128,576]{1,0:T(8,128)(2,1)S(1)}, bf16[128,576]{1,0:T(8,128)(2,1)S(1)}, u32[]{:S(2)}, u32[]{:S(2)}) collective-permute-start(bf16[128,576]{1,0:T(8,128)(2,1)S(1)} %add_convert_fusion.3), channel_id=1, source_target_pairs={{0,1},{1,0},{2,3},{3,2},{4,5},{5,4},{6,7},{7,6},{8,9},{9,8},{10,11... | collective-permute-start | bytes 442376 | tf_op jit(solution)/shard_map/ppermute | solution.py:54
  63.3 14.8 %collective-permute-start.7 = (bf16[128,576]{1,0:T(8,128)(2,1)S(1)}, bf16[128,576]{1,0:T(8,128)(2,1)S(1)}, u32[]{:S(2)}, u32[]{:S(2)}) collective-permute-start(bf16[128,576]{1,0:T(8,128)(2,1)S(1)} %add_convert_fusion.2), channel_id=1, source_target_pairs={{0,2},{1,3},{2,0},{3,1},{4,6},{5,7},{6,4},{7,5},{8,10},{9,11},{10,... | collective-permute-start | bytes 442376 | tf_op jit(solution)/shard_map/ppermute | solution.py:54
  78.2 10.6 %collective-permute-start.8 = (bf16[128,576]{1,0:T(8,128)(2,1)S(1)}, bf16[128,576]{1,0:T(8,128)(2,1)S(1)}, u32[]{:S(2)}, u32[]{:S(2)}) collective-permute-start(bf16[128,576]{1,0:T(8,128)(2,1)S(1)} %add_convert_fusion.1), channel_id=1, source_target_pairs={{0,4},{1,5},{2,6},{3,7},{4,0},{5,1},{6,2},{7,3},{8,12},{9,13},{10,... | collective-permute-start | bytes 442376 | tf_op jit(solution)/shard_map/ppermute | solution.py:54
